TPU v7x, 32 devices: a whole 2x2x4 slice. The times are simulated.
32 devices in a mesh: freq: 2 (over y), gx: 4 (over z), gy: 2 (over x), col: 2 (over core).
Axes of the slice: x: 2, y: 2, z: 4, core: 2. Of those that a mesh axis runs over, the one named last changes fastest.
Arguments:
- source: bfloat16 [12, 64, 32, 256], P('freq', 'gx', 'gy', 'col'), parts along dimension 0, may hold values from -6 to 6
- warm: bfloat16 [12, 64, 32, 256], P('freq', 'gx', 'gy', 'col'), parts along dimension 0, may hold values from -2.1 to 2.6
- forward: bfloat16 [12, 64, 32, 256], P('freq', 'gx', 'gy', 'col'), parts along dimension 0, may hold values from -6 to 6
- density: bfloat16 [64, 32, 256], P('gx', 'gy', 'col'), may hold values from 1 to 3
- material_map: int32 [8, 4, 8], P('gx', 'gy', 'col'), may hold values from 0 to 7
- material_table: float32 [8, 2], replicated, may hold values from 0.5 to 2
- iface_cells: int32 [16, 256], P(('gx', 'gy', 'col')), may hold values from 0 to 32767, as said below
- impedance: float32 [2, 3], replicated, may hold values from 2 to 8
- omega2: float32 [2], P('freq'), parts along dimension 0, may hold values from 0.5 to 1
Outputs:
- adjoint: float32 [12, 64, 32, 256], P('freq', 'gx', 'gy', 'col'), parts along dimension 0
- coarse_gradient: float32 [32, 8], P('freq'), parts along dimension 0
There are 2 independent parts, one for each index of `freq`. A program takes and returns all parts, laid end to end along the dimension named above; an argument that names none is the same for every part. Nothing has to cross between parts.
Inputs may be any that keep to these rules, and one draw needn't show every extreme that they name: `iface_cells`: each row's entries are distinct, rising, and within the tile of 16 x 16 x 128 cells; row r belongs to the device of that index along gx, gy and col together.
All inputs are finite; a program needn't handle non-finite values.
Results may differ from a plain program's by a relative error of at most 0.0003.
Values may be sent and summed in bfloat16 or wider, within the bound.
No kernel may reach another device: no remote copies, remote signals or barrier semaphores. Data moves between devices by JAX's collectives and lax.ppermute only.
A program may use at most 64 MiB of HBM per device.

v0:
```python
import jax
import jax.numpy as jnp
from jax import lax
from jax.sharding import PartitionSpec as P

DAMPING = 0.5
RELAXATION = 0.6


def with_halo(array, sides, width):
    for axis, dim in sides:
        peers, length = (lax.axis_size(axis), array.shape[dim])
        up = [(i, (i + 1) % peers) for i in range(peers - 1)]
        down = [(j, i) for i, j in up]
        last = lax.slice_in_dim(array, length - width, length, axis=dim)
        initial = lax.slice_in_dim(array, 0, width, axis=dim)
        before = lax.ppermute(last, axis, up)
        after = lax.ppermute(initial, axis, down)
        array = jnp.concatenate([before, array, after], axis=dim)
    return array


def window(padded, offset):
    size_x = padded.shape[1] - 2
    size_y = padded.shape[2] - 2
    size_z = padded.shape[3] - 2
    return padded[
        :,
        1 + offset[0] : 1 + offset[0] + size_x,
        1 + offset[1] : 1 + offset[1] + size_y,
        1 + offset[2] : 1 + offset[2] + size_z,
    ]


def navier(padded, lame_first, shear):
    units = ((1, 0, 0), (0, 1, 0), (0, 0, 1))
    centre = window(padded, (0, 0, 0))
    second = []
    for axis_d in range(3):
        ahead = units[axis_d]
        behind = tuple((-value for value in ahead))
        second.append(window(padded, ahead) + window(padded, behind) - 2.0 * centre)
    laplace = second[0] + second[1] + second[2]
    result = []
    for part_index in range(2):
        for component in range(3):
            channel = part_index * 3 + component
            divergence = second[component][channel]
            for other_axis in range(3):
                if other_axis != component:
                    source_channel = part_index * 3 + other_axis
                    single = padded[source_channel : source_channel + 1]
                    first_unit = units[component]
                    other_unit = units[other_axis]
                    plus_plus = tuple((first_unit[k] + other_unit[k] for k in range(3)))
                    plus_minus = tuple((first_unit[k] - other_unit[k] for k in range(3)))
                    minus_plus = tuple((-first_unit[k] + other_unit[k] for k in range(3)))
                    minus_minus = tuple((-first_unit[k] - other_unit[k] for k in range(3)))
                    mixed = (
                        window(single, plus_plus)
                        - window(single, plus_minus)
                        - window(single, minus_plus)
                        + window(single, minus_minus)
                    )
                    divergence = divergence + 0.25 * mixed[0]
            result.append(shear * laplace[channel] + (lame_first + shear) * divergence)
    return jnp.stack(result)


def sweep(padded, lame_first, shear, density, mask, source, mean_field, omega_sq, impedance):
    field = window(padded, (0, 0, 0))
    elastic = navier(padded, lame_first, shear)
    real_part = field[:3]
    imag_part = field[3:]
    mean_real = mean_field[:3][:, None, None, None]
    mean_imag = mean_field[3:][:, None, None, None]
    imp_real = impedance[0][:, None, None, None]
    imp_imag = impedance[1][:, None, None, None]
    inertia = omega_sq * density
    diff_real = real_part - mean_real
    diff_imag = imag_part - mean_imag
    apply_real = (
        -elastic[:3]
        - inertia * (real_part - DAMPING * imag_part)
        + mask * (imp_real * diff_real - imp_imag * diff_imag)
    )
    apply_imag = (
        -elastic[3:]
        - inertia * (imag_part + DAMPING * real_part)
        + mask * (imp_real * diff_imag + imp_imag * diff_real)
    )
    resid_real = source[:3] - apply_real
    resid_imag = source[3:] - apply_imag
    diag_real = 8.0 * shear + 2.0 * lame_first - inertia + mask * imp_real
    diag_imag = -DAMPING * inertia + mask * imp_imag
    modulus = diag_real * diag_real + diag_imag * diag_imag
    new_real = real_part + RELAXATION * (resid_real * diag_real + resid_imag * diag_imag) / modulus
    new_imag = imag_part + RELAXATION * (resid_imag * diag_real - resid_real * diag_imag) / modulus
    return jnp.concatenate([new_real, new_imag], 0)


def expand(blocks):
    blocks_x, blocks_y, blocks_z = blocks.shape
    spread = jnp.broadcast_to(
        blocks[:, None, :, None, :, None], (blocks_x, 8, blocks_y, 8, blocks_z, 32)
    )
    return spread.reshape(blocks_x * 8, blocks_y * 8, blocks_z * 32)


def material(block_ids, table):
    lame_first = jnp.zeros(block_ids.shape, jnp.float32)
    shear = jnp.zeros(block_ids.shape, jnp.float32)
    for entry in range(table.shape[0]):
        chosen = block_ids == entry
        lame_first = jnp.where(chosen, table[entry, 0], lame_first)
        shear = jnp.where(chosen, table[entry, 1], shear)
    return (lame_first, shear)


def foundation(field, mask, count):
    total = lax.psum(jnp.sum(mask * field, axis=(1, 2, 3)), ("gx", "gy", "col"))
    return total / count


def shards(
    source, warm, forward, density, material_map, material_table, iface_cells, impedance, omega2
):
    omega_sq = omega2[0]
    tile_shape = density.shape
    tile_cells = tile_shape[0] * tile_shape[1] * tile_shape[2]
    mask = jnp.zeros((tile_cells,), jnp.float32).at[iface_cells[0]].set(1.0).reshape(tile_shape)
    block_ids = expand(material_map)
    lame_first, shear = material(block_ids, material_table)
    density_cells = density.astype(jnp.float32)
    source_cells = source.astype(jnp.float32)
    group_size = lax.axis_size("gx") * lax.axis_size("gy") * lax.axis_size("col")
    count = jnp.float32(group_size * iface_cells.shape[1])
    field = warm.astype(jnp.float32)
    for sweep_index in range(2):
        mean_field = foundation(field, mask, count)
        padded = with_halo(field, (("gx", 1), ("gy", 2), ("col", 3)), 1)
        field = sweep(
            padded,
            lame_first,
            shear,
            density_cells,
            mask,
            source_cells,
            mean_field,
            omega_sq,
            impedance,
        )
    forward_cells = forward.astype(jnp.float32)
    correlation = (
        field[:3] * forward_cells[:3]
        - field[3:] * forward_cells[3:]
        - DAMPING * (field[:3] * forward_cells[3:] + field[3:] * forward_cells[:3])
    )
    cell_terms = -omega_sq * jnp.sum(correlation, axis=0)
    coarse_x = tile_shape[0] // 4
    coarse_y = tile_shape[1] // 4
    local_sums = cell_terms.reshape(coarse_x, 4, coarse_y, 4, tile_shape[2]).sum(axis=(1, 3, 4))
    paired = lax.psum(local_sums, "col")
    gathered = lax.all_gather(paired[None], ("gx", "gy"), axis=0, tiled=True)
    grid_sums = gathered.reshape(lax.axis_size("gx"), lax.axis_size("gy"), coarse_x, coarse_y)
    coarse = (
        grid_sums.transpose(0, 2, 1, 3).reshape(
            lax.axis_size("gx") * coarse_x, lax.axis_size("gy") * coarse_y
        )
        / 64.0
    )
    return (field, coarse)


def solution(mesh):
    in_specs = (
        P("freq", "gx", "gy", "col"),
        P("freq", "gx", "gy", "col"),
        P("freq", "gx", "gy", "col"),
        P("gx", "gy", "col"),
        P("gx", "gy", "col"),
        P(),
        P(("gx", "gy", "col"), None),
        P(),
        P("freq"),
    )
    out_specs = (P("freq", "gx", "gy", "col"), P("freq", None))
    return jax.shard_map(shards, mesh=mesh, in_specs=in_specs, out_specs=out_specs, check_vma=False)
```

profile of v0, /device:TPU:0, one launch (start us, length us, event | category | flops | bytes accessed | tf_op | source)
XLA Modules:
  0.0 208.3 jit_solution(2462226845284078183)
XLA Ops:
  2.7 5.6 %collective-permute-start.1 = (f32[6,1,16,128]{3,2,1,0:T(8,128)S(1)}, f32[6,1,16,128]{3,2,1,0:T(8,128)S(1)}, u32[]{:S(2)}, u32[]{:S(2)}) collective-permute-start(f32[6,1,16,128]{3,2,1,0:T(8,128)S(1)} %get-tuple-element.40), channel_id=1, source_target_pairs={{0,4},{4,8},{8,12},{1,5},{5,9},{9,13},{2,6},{6,10},{10,14},{3,7},{... | collective-permute-start | bytes 147464 | tf_op jit(solution)/shard_map/ppermute | solution.py:17
  8.3 2.0 fusion.108
  11.0 1.9 broadcast_select_fusion
  12.9 4.6 %select_select_fusion.1 = f32[2,8,2,8,4,32]{5,4,3,2,1,0:T(4,128)S(1)} fusion(f32[]{:T(128)} %bitcast, f32[]{:T(128)} %bitcast.1, f32[]{:T(128)} %bitcast.2, f32[]{:T(128)} %bitcast.3, f32[]{:T(128)} %bitcast.4, f32[2,2,4]{2,1,0:T(2,128)S(1)} %get-tuple-element.46, f32[]{:T(128)} %bitcast.6, f32[]{:T(128)} %bitcast.5, ...), kind=kLoop, calls=%fused_computation.41 | loop fusion | flops 229376 | bytes 131276 | tf_op jit(solution)/shard_map/jit(_where)/select_n | solution.py:116
  17.4 4.5 %select_select_fusion = f32[2,8,2,8,4,32]{5,4,3,2,1,0:T(4,128)S(1)} fusion(f32[]{:T(128)} %bitcast.8, f32[]{:T(128)} %bitcast.9, f32[]{:T(128)} %bitcast.10, f32[]{:T(128)} %bitcast.11, f32[]{:T(128)} %bitcast.12, f32[2,2,4]{2,1,0:T(2,128)S(1)} %get-tuple-element.45, f32[]{:T(128)} %bitcast.14, f32[]{:T(128)} %bitcast.13, ...), kind=kLoop, calls=%fused_computation.40 | loop fusion | flops 229376 | bytes 131276 | tf_op jit(solution)/shard_map/jit(_where)/select_n | solution.py:115
  22.0 8.9 %multiply_add_fusion = f32[2,8,2,8,4,32]{5,4,3,2,1,0:T(4,128)S(1)} fusion(f32[2,2,4]{2,1,0:T(2,128)S(1)} %get-tuple-element.46, f32[]{:T(128)} %bitcast.6, pred[2,2,4]{2,1,0:T(4,128)(4,1)S(1)} %get-tuple-element.53, f32[]{:T(128)} %bitcast.5, pred[2,2,4]{2,1,0:T(4,128)(4,1)S(1)} %get-tuple-element.48, f32[]{:T(128)} %bitcast.4, ...), kind=kLoop, calls=%fused_computation.39 | loop fusion | flops 557056 | bytes 131368 | tf_op jit(solution)/shard_map/add | solution.py:94
  34.1 5.8 %collective-permute-start.3 = (f32[6,18,1,128]{3,2,1,0:T(1,128)S(1)}, f32[6,18,1,128]{3,2,1,0:T(1,128)}, u32[]{:S(2)}, u32[]{:S(2)}) collective-permute-start(f32[6,18,1,128]{3,2,1,0:T(1,128)S(1)} %get-tuple-element.34), channel_id=1, source_target_pairs={{0,2},{1,3},{4,6},{5,7},{8,10},{9,11},{12,14},{13,15},{16,18},{17,... | collective-permute-start | bytes 165896 | tf_op jit(solution)/shard_map/ppermute | solution.py:17
  42.7 2.0 scatter_custom_fusion
  50.0 3.6 %collective-permute-start.5 = (f32[6,18,18,1]{2,1,3,0:T(8,128)S(1)}, f32[6,18,18,1]{2,1,3,0:T(8,128)}, u32[]{:S(2)}, u32[]{:S(2)}) collective-permute-start(f32[6,18,18,1]{2,1,3,0:T(8,128)S(1)} %copy.46), channel_id=1, source_target_pairs={{0,1},{2,3},{4,5},{6,7},{8,9},{10,11},{12,13},{14,15},{16,17},{18,... | collective-permute-start | bytes 23336 | tf_op jit(solution)/shard_map/ppermute | solution.py:17
  53.7 2.6 %pad_maximum_fusion.2 = (f32[6,18,17,128]{3,2,1,0:T(8,128)}, f32[6,18,17,128]{3,2,1,0:T(8,128)}) fusion(f32[6,18,1,128]{3,2,1,0:T(1,128)} %collective-permute-done.2, f32[6,1,16,128]{3,2,1,0:T(8,128)S(1)} %collective-permute-done, f32[6,16,16,128]{3,2,1,0:T(8,128)S(1)} %convert_element_type.12, f32[6,1,16,128]{3,2,1,0:T(8,128)S(1)} %collective-permute-done.1, ...), kind=kLoop, calls=%fused_computation.5 | loop fusion | flops 1410048 | bytes 2875392 | tf_op jit(solution)/shard_map/concatenate | solution.py:19
  58.7 3.1 %pad_maximum_fusion = (f32[6,18,18,129]{3,2,1,0:T(8,128)S(1)}, f32[6,18,18,129]{3,2,1,0:T(8,128)S(1)}) fusion(f32[6,18,18,1]{3,2,1,0:T(8,128)S(1)} %copy.45, f32[6,18,1,128]{3,2,1,0:T(1,128)} %collective-permute-done.2, f32[6,1,16,128]{3,2,1,0:T(8,128)S(1)} %collective-permute-done, f32[6,16,16,128]{3,2,1,0:T(8,128)S(1)} %convert_element_type.12, ...), kind=kLoop, calls=%fused_computation.1 | loop fusion | flops 2507760 | bytes 3017088 | tf_op jit(solution)/shard_map/concatenate | solution.py:19
  61.8 2.3 %add_add_fusion.1 = (f32[6,16,16,128]{3,2,1,0:T(8,128)}, f32[6,16,16,128]{3,2,1,0:T(8,128)}, f32[6,16,16,128]{3,2,1,0:T(8,128)}, f32[6,16,16,128]{3,2,1,0:T(8,128)}, f32[6]{0:T(128)S(1)}) fusion(bf16[6,16,16,128]{3,2,1,0:T(8,128)(2,1)S(1)} %copy-done.28, f32[6,18,17,128]{3,2,1,0:T(8,128)S(1)} %copy-done.17, f32[6,18,17,128]{3,2,1,0:T(8,128)S(1)} %copy-done.16, ...), kind=kLoop, calls=%fused_computation.38 | loop fusion | flops 2949114 | bytes 7700504 | tf_op jit(solution)/shard_map/add | solution.py:43
  64.2 29.5 %psum.21 = f32[6]{0:T(128)S(1)} all-reduce(f32[6]{0:T(128)S(1)} %get-tuple-element.39), channel_id=1, replica_groups=mesh['freq'=2,'gx'=4,'gy'=2,'col'=2] {'gx','gy','col'}, use_global_device_ids=true, to_apply=%region_2.3 | all-reduce | flops 6 | bytes 48 | tf_op jit(solution)/shard_map/psum | solution.py:121
  99.7 1.7 fusion.77
  101.5 1.7 fusion.59
  105.5 4.5 %collective-permute-start.7 = (f32[6,1,16,128]{3,2,1,0:T(8,128)S(1)}, f32[6,1,16,128]{3,2,1,0:T(8,128)S(1)}, u32[]{:S(2)}, u32[]{:S(2)}) collective-permute-start(f32[6,1,16,128]{3,2,1,0:T(8,128)S(1)} %get-tuple-element.37), channel_id=1, source_target_pairs={{0,4},{4,8},{8,12},{1,5},{5,9},{9,13},{2,6},{6,10},{10,14},{3,7},{... | collective-permute-start | bytes 147464 | tf_op jit(solution)/shard_map/ppermute | solution.py:17
  113.2 4.7 %collective-permute-start.9 = (f32[6,18,1,128]{3,2,1,0:T(1,128)S(1)}, f32[6,18,1,128]{3,2,1,0:T(1,128)S(1)}, u32[]{:S(2)}, u32[]{:S(2)}) collective-permute-start(f32[6,18,1,128]{3,2,1,0:T(1,128)S(1)} %get-tuple-element.30), channel_id=1, source_target_pairs={{0,2},{1,3},{4,6},{5,7},{8,10},{9,11},{12,14},{13,15},{16,18},{17,... | collective-permute-start | bytes 165896 | tf_op jit(solution)/shard_map/ppermute | solution.py:17
  124.8 3.6 %collective-permute-start.11 = (f32[6,18,18,1]{2,1,3,0:T(8,128)S(1)}, f32[6,18,18,1]{2,1,3,0:T(8,128)}, u32[]{:S(2)}, u32[]{:S(2)}) collective-permute-start(f32[6,18,18,1]{2,1,3,0:T(8,128)S(1)} %copy.50), channel_id=1, source_target_pairs={{0,1},{2,3},{4,5},{6,7},{8,9},{10,11},{12,13},{14,15},{16,17},{18,... | collective-permute-start | bytes 23336 | tf_op jit(solution)/shard_map/ppermute | solution.py:17
  128.4 1.7 pad_maximum_fusion.4
  132.6 3.6 %pad_maximum_fusion.1 = (f32[6,18,18,129]{3,2,1,0:T(8,128)S(1)}, f32[6,18,18,129]{3,2,1,0:T(8,128)S(1)}) fusion(f32[6,18,18,1]{3,2,1,0:T(8,128)S(1)} %copy.49, f32[6,18,1,128]{3,2,1,0:T(1,128)} %copy-done.10, f32[6,1,16,128]{3,2,1,0:T(8,128)S(1)} %collective-permute-done.6, f32[3,16,16,128]{3,2,1,0:T(8,128)S(1)} %divide_add_fusion.2, ...), kind=kLoop, calls=%fused_computation.3 | loop fusion | flops 3009312 | bytes 3017088 | tf_op jit(solution)/shard_map/concatenate | solution.py:19
  136.3 2.3 %add_add_fusion = (f32[6,16,16,128]{3,2,1,0:T(8,128)}, f32[6,16,16,128]{3,2,1,0:T(8,128)}, f32[6,16,16,128]{3,2,1,0:T(8,128)}, f32[6,16,16,128]{3,2,1,0:T(8,128)}, f32[6]{0:T(128)S(1)}) fusion(f32[3,16,16,128]{3,2,1,0:T(8,128)S(1)} %divide_add_fusion.2, f32[3,16,16,128]{3,2,1,0:T(8,128)S(1)} %get-tuple-element.11, f32[6,18,17,128]{3,2,1,0:T(8,128)S(1)} %copy-done.19, ...), kind=kLoop, calls=%fused_computation.36 | loop fusion | flops 3145722 | bytes 7307288 | tf_op jit(solution)/shard_map/add | solution.py:43
  138.6 29.5 %psum.22 = f32[6]{0:T(128)S(1)} all-reduce(f32[6]{0:T(128)S(1)} %get-tuple-element.36), channel_id=1, replica_groups=mesh['freq'=2,'gx'=4,'gy'=2,'col'=2] {'gx','gy','col'}, use_global_device_ids=true, to_apply=%region_4.5 | all-reduce | flops 6 | bytes 48 | tf_op jit(solution)/shard_map/psum | solution.py:121
  178.1 2.4 %psum.23 = f32[1,4,4]{2,1,0:T(4,128)S(1)} all-reduce(f32[1,4,4]{2,1,0:T(4,128)S(1)} %bitcast.39), channel_id=1, replica_groups=mesh['freq'=2,'gx'=4,'gy'=2,'col'=2] {'col'}, use_global_device_ids=true, to_apply=%region_8.9 | all-reduce | flops 16 | bytes 128 | tf_op jit(solution)/shard_map/psum | solution.py:163
  180.5 26.0 %all_gather.3 = f32[8,4,4]{2,1,0:T(4,128)S(1)} all-gather(f32[1,4,4]{2,1,0:T(4,128)S(1)} %psum.23), channel_id=1, replica_groups=mesh['freq'=2,'gx'=4,'gy'=2,'col'=2] {'gx','gy'}, dimensions={0}, use_global_device_ids=true | all-gather | bytes 576 | tf_op jit(solution)/shard_map/all_gather | solution.py:164
  (141 shorter events, 48.0 us)
Async XLA Ops:
  0.6 31.2 %copy-start.33 = (bf16[16,16,128]{2,1,0:T(8,128)(2,1)S(1)}, bf16[16,16,128]{2,1,0:T(8,128)(2,1)}, u32[]{:S(2)}) copy-start(bf16[16,16,128]{2,1,0:T(8,128)(2,1)} %param.12) | copy-start | bytes 196612
  1.4 31.2 %collective-permute-start = (f32[6,1,16,128]{3,2,1,0:T(8,128)S(1)}, f32[6,1,16,128]{3,2,1,0:T(8,128)S(1)}, u32[]{:S(2)}, u32[]{:S(2)}) collective-permute-start(f32[6,1,16,128]{3,2,1,0:T(8,128)S(1)} %get-tuple-element.41), channel_id=1, source_target_pairs={{4,0},{8,4},{12,8},{5,1},{9,5},{13,9},{6,2},{10,6},{14,10},{7,3},{... | collective-permute-start | bytes 147464 | tf_op jit(solution)/shard_map/ppermute | solution.py:18
  2.7 30.0 %collective-permute-start.1 = (f32[6,1,16,128]{3,2,1,0:T(8,128)S(1)}, f32[6,1,16,128]{3,2,1,0:T(8,128)S(1)}, u32[]{:S(2)}, u32[]{:S(2)}) collective-permute-start(f32[6,1,16,128]{3,2,1,0:T(8,128)S(1)} %get-tuple-element.40), channel_id=1, source_target_pairs={{0,4},{4,8},{8,12},{1,5},{5,9},{9,13},{2,6},{6,10},{10,14},{3,7},{... | collective-permute-start | bytes 147464 | tf_op jit(solution)/shard_map/ppermute | solution.py:17
  12.9 19.7 %copy-start.34 = (s32[1,256]{1,0:T(1,128)S(1)}, s32[1,256]{1,0:T(1,128)}, u32[]{:S(2)}) copy-start(s32[1,256]{1,0:T(1,128)} %param.15) | copy-start | bytes 3076
  12.9 19.7 %copy-start.27 = (bf16[6,16,16,128]{3,2,1,0:T(8,128)(2,1)S(1)}, bf16[6,16,16,128]{3,2,1,0:T(8,128)(2,1)}, u32[]{:S(2)}) copy-start(bf16[6,16,16,128]{3,2,1,0:T(8,128)(2,1)} %param.10) | copy-start | bytes 1179652
  31.8 8.1 %copy-start.35 = (f32[2,3]{1,0:T(2,128)S(1)}, f32[2,3]{1,0:T(2,128)}, u32[]{:S(2)}) copy-start(f32[2,3]{1,0:T(2,128)} %param.16) | copy-start | bytes 76
  32.7 9.0 %copy-start.31 = (bf16[6,16,16,128]{3,2,1,0:T(8,128)(2,1)S(1)}, bf16[6,16,16,128]{3,2,1,0:T(8,128)(2,1)}, u32[]{:S(2)}) copy-start(bf16[6,16,16,128]{3,2,1,0:T(8,128)(2,1)} %param.9) | copy-start | bytes 1179652
  32.8 11.9 %collective-permute-start.2 = (f32[6,18,1,128]{3,2,1,0:T(1,128)S(1)}, f32[6,18,1,128]{3,2,1,0:T(1,128)}, u32[]{:S(2)}, u32[]{:S(2)}) collective-permute-start(f32[6,18,1,128]{3,2,1,0:T(1,128)S(1)} %get-tuple-element.35), channel_id=1, source_target_pairs={{2,0},{3,1},{6,4},{7,5},{10,8},{11,9},{14,12},{15,13},{18,16},{19,... | collective-permute-start | bytes 165896 | tf_op jit(solution)/shard_map/ppermute | solution.py:18
  34.1 10.6 %collective-permute-start.3 = (f32[6,18,1,128]{3,2,1,0:T(1,128)S(1)}, f32[6,18,1,128]{3,2,1,0:T(1,128)}, u32[]{:S(2)}, u32[]{:S(2)}) collective-permute-start(f32[6,18,1,128]{3,2,1,0:T(1,128)S(1)} %get-tuple-element.34), channel_id=1, source_target_pairs={{0,2},{1,3},{4,6},{5,7},{8,10},{9,11},{12,14},{13,15},{16,18},{17,... | collective-permute-start | bytes 165896 | tf_op jit(solution)/shard_map/ppermute | solution.py:17
  47.8 8.5 %collective-permute-start.4 = (f32[6,18,18,1]{2,1,3,0:T(8,128)}, f32[6,18,18,1]{2,1,3,0:T(8,128)S(1)}, u32[]{:S(2)}, u32[]{:S(2)}) collective-permute-start(f32[6,18,18,1]{2,1,3,0:T(8,128)} %copy.44), channel_id=1, source_target_pairs={{1,0},{3,2},{5,4},{7,6},{9,8},{11,10},{13,12},{15,14},{17,16},{19,... | collective-permute-start | bytes 23336 | tf_op jit(solution)/shard_map/ppermute | solution.py:18
  50.0 7.0 %collective-permute-start.5 = (f32[6,18,18,1]{2,1,3,0:T(8,128)S(1)}, f32[6,18,18,1]{2,1,3,0:T(8,128)}, u32[]{:S(2)}, u32[]{:S(2)}) collective-permute-start(f32[6,18,18,1]{2,1,3,0:T(8,128)S(1)} %copy.46), channel_id=1, source_target_pairs={{0,1},{2,3},{4,5},{6,7},{8,9},{10,11},{12,13},{14,15},{16,17},{18,... | collective-permute-start | bytes 23336 | tf_op jit(solution)/shard_map/ppermute | solution.py:17
  95.3 6.1 %copy-start.2 = (f32[1,16,16,128]{3,2,1,0:T(8,128)}, f32[1,16,16,128]{3,2,1,0:T(8,128)S(1)}, u32[]{:S(2)}) copy-start(f32[1,16,16,128]{3,2,1,0:T(8,128)S(1)} %get-tuple-element.15) | copy-start | bytes 393220
  104.1 13.9 %copy-start.32 = (bf16[6,16,16,128]{3,2,1,0:T(8,128)(2,1)S(1)}, bf16[6,16,16,128]{3,2,1,0:T(8,128)(2,1)}, u32[]{:S(2)}) copy-start(bf16[6,16,16,128]{3,2,1,0:T(8,128)(2,1)} %param.11) | copy-start | bytes 1179652
  104.1 6.1 %collective-permute-start.6 = (f32[6,1,16,128]{3,2,1,0:T(8,128)S(1)}, f32[6,1,16,128]{3,2,1,0:T(8,128)S(1)}, u32[]{:S(2)}, u32[]{:S(2)}) collective-permute-start(f32[6,1,16,128]{3,2,1,0:T(8,128)S(1)} %get-tuple-element.38), channel_id=1, source_target_pairs={{4,0},{8,4},{12,8},{5,1},{9,5},{13,9},{6,2},{10,6},{14,10},{7,3},{... | collective-permute-start | bytes 147464 | tf_op jit(solution)/shard_map/ppermute | solution.py:18
  105.5 6.3 %collective-permute-start.7 = (f32[6,1,16,128]{3,2,1,0:T(8,128)S(1)}, f32[6,1,16,128]{3,2,1,0:T(8,128)S(1)}, u32[]{:S(2)}, u32[]{:S(2)}) collective-permute-start(f32[6,1,16,128]{3,2,1,0:T(8,128)S(1)} %get-tuple-element.37), channel_id=1, source_target_pairs={{0,4},{4,8},{8,12},{1,5},{5,9},{9,13},{2,6},{6,10},{10,14},{3,7},{... | collective-permute-start | bytes 147464 | tf_op jit(solution)/shard_map/ppermute | solution.py:17
  111.9 7.0 %collective-permute-start.8 = (f32[6,18,1,128]{3,2,1,0:T(1,128)S(1)}, f32[6,18,1,128]{3,2,1,0:T(1,128)S(1)}, u32[]{:S(2)}, u32[]{:S(2)}) collective-permute-start(f32[6,18,1,128]{3,2,1,0:T(1,128)S(1)} %get-tuple-element.31), channel_id=1, source_target_pairs={{2,0},{3,1},{6,4},{7,5},{10,8},{11,9},{14,12},{15,13},{18,16},{19,... | collective-permute-start | bytes 165896 | tf_op jit(solution)/shard_map/ppermute | solution.py:18
  113.2 6.3 %collective-permute-start.9 = (f32[6,18,1,128]{3,2,1,0:T(1,128)S(1)}, f32[6,18,1,128]{3,2,1,0:T(1,128)S(1)}, u32[]{:S(2)}, u32[]{:S(2)}) collective-permute-start(f32[6,18,1,128]{3,2,1,0:T(1,128)S(1)} %get-tuple-element.30), channel_id=1, source_target_pairs={{0,2},{1,3},{4,6},{5,7},{8,10},{9,11},{12,14},{13,15},{16,18},{17,... | collective-permute-start | bytes 165896 | tf_op jit(solution)/shard_map/ppermute | solution.py:17
  122.4 6.0 %copy-start.11 = (f32[6,18,1,128]{3,2,1,0:T(1,128)S(1)}, f32[6,18,1,128]{3,2,1,0:T(1,128)}, u32[]{:S(2)}) copy-start(f32[6,18,1,128]{3,2,1,0:T(1,128)} %copy-done.10) | copy-start | bytes 165892
  122.4 6.0 %copy-start.14 = (f32[6,18,1,128]{3,2,1,0:T(1,128)S(1)}, f32[6,18,1,128]{3,2,1,0:T(1,128)}, u32[]{:S(2)}) copy-start(f32[6,18,1,128]{3,2,1,0:T(1,128)} %copy-done.13) | copy-start | bytes 165892
  122.4 7.8 %collective-permute-start.10 = (f32[6,18,18,1]{2,1,3,0:T(8,128)}, f32[6,18,18,1]{2,1,3,0:T(8,128)S(1)}, u32[]{:S(2)}, u32[]{:S(2)}) collective-permute-start(f32[6,18,18,1]{2,1,3,0:T(8,128)} %copy.48), channel_id=1, source_target_pairs={{1,0},{3,2},{5,4},{7,6},{9,8},{11,10},{13,12},{15,14},{17,16},{19,... | collective-permute-start | bytes 23336 | tf_op jit(solution)/shard_map/ppermute | solution.py:18
  124.8 6.2 %collective-permute-start.11 = (f32[6,18,18,1]{2,1,3,0:T(8,128)S(1)}, f32[6,18,18,1]{2,1,3,0:T(8,128)}, u32[]{:S(2)}, u32[]{:S(2)}) collective-permute-start(f32[6,18,18,1]{2,1,3,0:T(8,128)S(1)} %copy.50), channel_id=1, source_target_pairs={{0,1},{2,3},{4,5},{6,7},{8,9},{10,11},{12,13},{14,15},{16,17},{18,... | collective-permute-start | bytes 23336 | tf_op jit(solution)/shard_map/ppermute | solution.py:17
  132.6 3.7 %copy-start.8 = (f32[32768]{0:T(1024)S(1)}, f32[32768]{0:T(1024)}, u32[]{:S(2)}) copy-start(f32[32768]{0:T(1024)} %scatter_custom_fusion) | copy-start | bytes 393220
  132.6 3.7 %copy-start.18 = (f32[6,18,17,128]{3,2,1,0:T(8,128)S(1)}, f32[6,18,17,128]{3,2,1,0:T(8,128)}, u32[]{:S(2)}) copy-start(f32[6,18,17,128]{3,2,1,0:T(8,128)} %get-tuple-element.28) | copy-start | bytes 2820100
  132.6 3.7 %copy-start.19 = (f32[6,18,17,128]{3,2,1,0:T(8,128)S(1)}, f32[6,18,17,128]{3,2,1,0:T(8,128)}, u32[]{:S(2)}) copy-start(f32[6,18,17,128]{3,2,1,0:T(8,128)} %get-tuple-element.29) | copy-start | bytes 2820100
  (24 other events, 44.8 us)
where the time goes:
time: 210 us; the launch traced here: 208 us
  blocking collectives  87.4 us (42%)
  other arithmetic  61.2 us (29%)
  starting transfers between devices  35.9 us (17%)
  local copies, waits for them, and re-layouts  19.4 us (9%)
  waiting for transfers between devices  2.4 us (1%)
    psum x2, blocking collectives, foundation(): total = lax.psum(jnp.sum(mask * field, axis=(1, 2, 3)), ('gx', 'gy', 'col'))  58.9 us
    ppermute x6, starting transfers between devices, with_halo(): before = lax.ppermute(last, axis, up)  27.9 us
    all_gather x1, blocking collectives, shards(): gathered = lax.all_gather(paired[None], ('gx', 'gy'), axis=0, tiled=True)  26 us
    add x12, other arithmetic, navier(): result.append(shear * laplace[channel] + (lame_first + shear) * divergence)  18.1 us
    concatenate x8, other arithmetic, with_halo(): array = jnp.concatenate([before, array, after], axis=dim)  12.4 us
    add x1, other arithmetic, sweep(): diag_real = 8.0 * shear + 2.0 * lame_first - inertia + mask * imp_real  8.89 us
    ppermute x6, starting transfers between devices, with_halo(): after = lax.ppermute(initial, axis, down)  7.99 us
    select_n x2, other arithmetic, material(): lame_first = jnp.where(chosen, table[entry, 0], lame_first)  6.44 us
  transfers between devices with their start and end apart: 12, of which 3 were waited for; matrix products, arithmetic and copies ran while one was open for 18% of the time, Pallas kernels for 0%

commit v1 on v0

--- a/solution.py
+++ b/solution.py
@@ -118,7 +118,9 @@
 
 
 def foundation(field, mask, count):
-    total = lax.psum(jnp.sum(mask * field, axis=(1, 2, 3)), ("gx", "gy", "col"))
+    total = jnp.sum(mask * field, axis=(1, 2, 3))
+    for over in (("gy", "col"), "gx"):
+        total = lax.psum(total, over)
     return total / count
 
 

time: 210 us -> 185 us (0.88)
  blocking collectives: 87.4 us -> 61.5 us
    psum x2 -> x4, blocking collectives: 58.9 us -> 33.1 us  [foundation(): total = lax.psum(total, over)]
  transfers between devices with their start and end apart: 12 -> 12, of which waited for: 3 -> 3; matrix products, arithmetic and copies ran while one was open for 18% -> 20% of each run, Pallas kernels for 0% -> 0%
where the time goes in v1:
time: 185 us; the launch traced here: 183 us
  other arithmetic  62 us (34%)
  blocking collectives  61.5 us (33%)
  starting transfers between devices  35.9 us (19%)
  local copies, waits for them, and re-layouts  19.4 us (10%)
  waiting for transfers between devices  2.4 us (1%)
  between operations  1.98 us (1%)
    psum x4, blocking collectives, foundation(): total = lax.psum(total, over)  33.1 us
    ppermute x6, starting transfers between devices, with_halo(): before = lax.ppermute(last, axis, up)  27.9 us
    all_gather x1, blocking collectives, shards(): gathered = lax.all_gather(paired[None], ('gx', 'gy'), axis=0, tiled=True)  26 us
    add x12, other arithmetic, navier(): result.append(shear * laplace[channel] + (lame_first + shear) * divergence)  18.1 us
    concatenate x8, other arithmetic, with_halo(): array = jnp.concatenate([before, array, after], axis=dim)  12.4 us
    add x1, other arithmetic, sweep(): diag_real = 8.0 * shear + 2.0 * lame_first - inertia + mask * imp_real  8.78 us
    ppermute x6, starting transfers between devices, with_halo(): after = lax.ppermute(initial, axis, down)  7.99 us
    select_n x2, other arithmetic, material(): lame_first = jnp.where(chosen, table[entry, 0], lame_first)  6.51 us
  transfers between devices with their start and end apart: 12, of which 3 were waited for; matrix products, arithmetic and copies ran while one was open for 20% of the time, Pallas kernels for 0%

profile of v1, /device:TPU:0, one launch (start us, length us, event | category | flops | bytes accessed | tf_op | source)
XLA Modules:
  0.0 183.2 jit_solution(7849595298388787738)
XLA Ops:
  2.7 5.6 %collective-permute-start.1 = (f32[6,1,16,128]{3,2,1,0:T(8,128)S(1)}, f32[6,1,16,128]{3,2,1,0:T(8,128)S(1)}, u32[]{:S(2)}, u32[]{:S(2)}) collective-permute-start(f32[6,1,16,128]{3,2,1,0:T(8,128)S(1)} %get-tuple-element.40), channel_id=1, source_target_pairs={{0,4},{4,8},{8,12},{1,5},{5,9},{9,13},{2,6},{6,10},{10,14},{3,7},{... | collective-permute-start | bytes 147464 | tf_op jit(solution)/shard_map/ppermute | solution.py:17
  8.3 2.0 %fusion.108 = (f32[1,1]{0,1:T(1,128)}, f32[1,1]{0,1:T(1,128)}, f32[1,1]{0,1:T(1,128)}, f32[1,1]{0,1:T(1,128)}, f32[1,1]{0,1:T(1,128)}, /*index=5*/f32[1,1]{0,1:T...) fusion(f32[8,2]{0,1:T(2,128)} %param.14), kind=kLoop, calls=%fused_computation.256 | loop fusion | bytes 128 | tf_op jit(solution)/shard_map/slice | solution.py:115
  11.0 2.0 %broadcast_select_fusion = (f32[2,2,4]{2,1,0:T(2,128)S(1)}, f32[2,2,4]{2,1,0:T(2,128)S(1)}) fusion(f32[]{:T(128)} %bitcast.15, s32[2,2,4]{2,1,0:T(2,128)} %param.13, f32[]{:T(128)} %bitcast.7), kind=kLoop, calls=%fused_computation.239 | loop fusion | flops 48 | bytes 200 | tf_op jit(solution)/shard_map/jit(_where)/select_n | solution.py:115
  12.9 4.4 %select_select_fusion.1 = f32[2,8,2,8,4,32]{5,4,3,2,1,0:T(4,128)S(1)} fusion(f32[]{:T(128)} %bitcast, f32[]{:T(128)} %bitcast.1, f32[]{:T(128)} %bitcast.2, f32[]{:T(128)} %bitcast.3, f32[]{:T(128)} %bitcast.4, f32[2,2,4]{2,1,0:T(2,128)S(1)} %get-tuple-element.46, f32[]{:T(128)} %bitcast.6, f32[]{:T(128)} %bitcast.5, ...), kind=kLoop, calls=%fused_computation.41 | loop fusion | flops 229376 | bytes 131276 | tf_op jit(solution)/shard_map/jit(_where)/select_n | solution.py:116
  17.4 4.6 %select_select_fusion = f32[2,8,2,8,4,32]{5,4,3,2,1,0:T(4,128)S(1)} fusion(f32[]{:T(128)} %bitcast.8, f32[]{:T(128)} %bitcast.9, f32[]{:T(128)} %bitcast.10, f32[]{:T(128)} %bitcast.11, f32[]{:T(128)} %bitcast.12, f32[2,2,4]{2,1,0:T(2,128)S(1)} %get-tuple-element.45, f32[]{:T(128)} %bitcast.14, f32[]{:T(128)} %bitcast.13, ...), kind=kLoop, calls=%fused_computation.40 | loop fusion | flops 229376 | bytes 131276 | tf_op jit(solution)/shard_map/jit(_where)/select_n | solution.py:115
  21.9 8.8 %multiply_add_fusion = f32[2,8,2,8,4,32]{5,4,3,2,1,0:T(4,128)S(1)} fusion(f32[2,2,4]{2,1,0:T(2,128)S(1)} %get-tuple-element.46, f32[]{:T(128)} %bitcast.6, pred[2,2,4]{2,1,0:T(4,128)(4,1)S(1)} %get-tuple-element.53, f32[]{:T(128)} %bitcast.5, pred[2,2,4]{2,1,0:T(4,128)(4,1)S(1)} %get-tuple-element.48, f32[]{:T(128)} %bitcast.4, ...), kind=kLoop, calls=%fused_computation.39 | loop fusion | flops 557056 | bytes 131368 | tf_op jit(solution)/shard_map/add | solution.py:94
  33.9 5.8 %collective-permute-start.3 = (f32[6,18,1,128]{3,2,1,0:T(1,128)S(1)}, f32[6,18,1,128]{3,2,1,0:T(1,128)}, u32[]{:S(2)}, u32[]{:S(2)}) collective-permute-start(f32[6,18,1,128]{3,2,1,0:T(1,128)S(1)} %get-tuple-element.34), channel_id=1, source_target_pairs={{0,2},{1,3},{4,6},{5,7},{8,10},{9,11},{12,14},{13,15},{16,18},{17,... | collective-permute-start | bytes 165896 | tf_op jit(solution)/shard_map/ppermute | solution.py:17
  41.5 2.0 %scatter_custom_fusion = f32[32768]{0:T(1024)} fusion(s32[256]{0:T(256)S(1)} %bitcast.40, f32[256]{0:T(256)S(1)} %broadcast.754, f32[]{:T(128)} %constant.7.clone.1), kind=kCustom, calls=%fused_computation.225 | custom fusion | bytes 131076 | tf_op jit(solution)/shard_map/scatter | solution.py:133
  48.8 3.7 %collective-permute-start.5 = (f32[6,18,18,1]{2,1,3,0:T(8,128)S(1)}, f32[6,18,18,1]{2,1,3,0:T(8,128)}, u32[]{:S(2)}, u32[]{:S(2)}) collective-permute-start(f32[6,18,18,1]{2,1,3,0:T(8,128)S(1)} %copy.46), channel_id=1, source_target_pairs={{0,1},{2,3},{4,5},{6,7},{8,9},{10,11},{12,13},{14,15},{16,17},{18,... | collective-permute-start | bytes 23336 | tf_op jit(solution)/shard_map/ppermute | solution.py:17
  52.5 2.6 %pad_maximum_fusion.2 = (f32[6,18,17,128]{3,2,1,0:T(8,128)}, f32[6,18,17,128]{3,2,1,0:T(8,128)}) fusion(f32[6,18,1,128]{3,2,1,0:T(1,128)} %collective-permute-done.2, f32[6,1,16,128]{3,2,1,0:T(8,128)S(1)} %collective-permute-done, f32[6,16,16,128]{3,2,1,0:T(8,128)S(1)} %convert_element_type.12, f32[6,1,16,128]{3,2,1,0:T(8,128)S(1)} %collective-permute-done.1, ...), kind=kLoop, calls=%fused_computation.5 | loop fusion | flops 1410048 | bytes 2875392 | tf_op jit(solution)/shard_map/concatenate | solution.py:19
  57.5 3.1 %pad_maximum_fusion = (f32[6,18,18,129]{3,2,1,0:T(8,128)S(1)}, f32[6,18,18,129]{3,2,1,0:T(8,128)S(1)}) fusion(f32[6,18,18,1]{3,2,1,0:T(8,128)S(1)} %copy.45, f32[6,18,1,128]{3,2,1,0:T(1,128)} %collective-permute-done.2, f32[6,1,16,128]{3,2,1,0:T(8,128)S(1)} %collective-permute-done, f32[6,16,16,128]{3,2,1,0:T(8,128)S(1)} %convert_element_type.12, ...), kind=kLoop, calls=%fused_computation.1 | loop fusion | flops 2507760 | bytes 3017088 | tf_op jit(solution)/shard_map/concatenate | solution.py:19
  60.6 2.3 %add_add_fusion.1 = (f32[6,16,16,128]{3,2,1,0:T(8,128)}, f32[6,16,16,128]{3,2,1,0:T(8,128)}, f32[6,16,16,128]{3,2,1,0:T(8,128)}, f32[6,16,16,128]{3,2,1,0:T(8,128)}, f32[6]{0:T(128)S(1)}) fusion(bf16[6,16,16,128]{3,2,1,0:T(8,128)(2,1)S(1)} %copy-done.28, f32[6,18,17,128]{3,2,1,0:T(8,128)S(1)} %copy-done.17, f32[6,18,17,128]{3,2,1,0:T(8,128)S(1)} %copy-done.16, ...), kind=kLoop, calls=%fused_computation.38 | loop fusion | flops 2949114 | bytes 7700504 | tf_op jit(solution)/shard_map/add | solution.py:43
  62.9 5.7 %psum.35 = f32[6]{0:T(128)S(1)} all-reduce(f32[6]{0:T(128)S(1)} %get-tuple-element.39), channel_id=1, replica_groups=mesh['freq'=2,'gx'=4,'gy'=2,'col'=2] {'gy','col'}, use_global_device_ids=true, to_apply=%region_2.3 | all-reduce | flops 6 | bytes 48 | tf_op jit(solution)/shard_map/psum | solution.py:123
  68.7 2.0 %convert_element_type.13 = f32[6,16,16,128]{3,2,1,0:T(8,128)} convert(bf16[6,16,16,128]{3,2,1,0:T(8,128)(2,1)} %param.9) | non-fusion elementwise | flops 196608 | bytes 1179648 | tf_op jit(solution)/shard_map/convert_element_type | solution.py:137
  70.7 10.3 %psum.36 = f32[6]{0:T(128)S(1)} all-reduce(f32[6]{0:T(128)S(1)} %psum.35), channel_id=1, replica_groups=mesh['freq'=2,'gx'=4,'gy'=2,'col'=2] {'gx'}, use_global_device_ids=true, to_apply=%region_3.4 | all-reduce | flops 6 | bytes 48 | tf_op jit(solution)/shard_map/psum | solution.py:123
  93.0 4.5 %collective-permute-start.7 = (f32[6,1,16,128]{3,2,1,0:T(8,128)S(1)}, f32[6,1,16,128]{3,2,1,0:T(8,128)S(1)}, u32[]{:S(2)}, u32[]{:S(2)}) collective-permute-start(f32[6,1,16,128]{3,2,1,0:T(8,128)S(1)} %get-tuple-element.37), channel_id=1, source_target_pairs={{0,4},{4,8},{8,12},{1,5},{5,9},{9,13},{2,6},{6,10},{10,14},{3,7},{... | collective-permute-start | bytes 147464 | tf_op jit(solution)/shard_map/ppermute | solution.py:17
  100.6 4.7 %collective-permute-start.9 = (f32[6,18,1,128]{3,2,1,0:T(1,128)S(1)}, f32[6,18,1,128]{3,2,1,0:T(1,128)S(1)}, u32[]{:S(2)}, u32[]{:S(2)}) collective-permute-start(f32[6,18,1,128]{3,2,1,0:T(1,128)S(1)} %get-tuple-element.30), channel_id=1, source_target_pairs={{0,2},{1,3},{4,6},{5,7},{8,10},{9,11},{12,14},{13,15},{16,18},{17,... | collective-permute-start | bytes 165896 | tf_op jit(solution)/shard_map/ppermute | solution.py:17
  112.2 3.7 %collective-permute-start.11 = (f32[6,18,18,1]{2,1,3,0:T(8,128)S(1)}, f32[6,18,18,1]{2,1,3,0:T(8,128)}, u32[]{:S(2)}, u32[]{:S(2)}) collective-permute-start(f32[6,18,18,1]{2,1,3,0:T(8,128)S(1)} %copy.50), channel_id=1, source_target_pairs={{0,1},{2,3},{4,5},{6,7},{8,9},{10,11},{12,13},{14,15},{16,17},{18,... | collective-permute-start | bytes 23336 | tf_op jit(solution)/shard_map/ppermute | solution.py:17
  120.0 3.6 %pad_maximum_fusion.1 = (f32[6,18,18,129]{3,2,1,0:T(8,128)S(1)}, f32[6,18,18,129]{3,2,1,0:T(8,128)S(1)}) fusion(f32[6,18,18,1]{3,2,1,0:T(8,128)S(1)} %copy.49, f32[6,18,1,128]{3,2,1,0:T(1,128)} %copy-done.10, f32[6,1,16,128]{3,2,1,0:T(8,128)S(1)} %collective-permute-done.6, f32[3,16,16,128]{3,2,1,0:T(8,128)S(1)} %divide_add_fusion.2, ...), kind=kLoop, calls=%fused_computation.3 | loop fusion | flops 3009312 | bytes 3017088 | tf_op jit(solution)/shard_map/concatenate | solution.py:19
  123.7 2.3 %add_add_fusion = (f32[6,16,16,128]{3,2,1,0:T(8,128)}, f32[6,16,16,128]{3,2,1,0:T(8,128)}, f32[6,16,16,128]{3,2,1,0:T(8,128)}, f32[6,16,16,128]{3,2,1,0:T(8,128)}, f32[6]{0:T(128)S(1)}) fusion(f32[3,16,16,128]{3,2,1,0:T(8,128)S(1)} %divide_add_fusion.2, f32[3,16,16,128]{3,2,1,0:T(8,128)S(1)} %get-tuple-element.11, f32[6,18,17,128]{3,2,1,0:T(8,128)S(1)} %copy-done.19, ...), kind=kLoop, calls=%fused_computation.36 | loop fusion | flops 3145722 | bytes 7307288 | tf_op jit(solution)/shard_map/add | solution.py:43
  126.0 6.3 %psum.37 = f32[6]{0:T(128)S(1)} all-reduce(f32[6]{0:T(128)S(1)} %get-tuple-element.36), channel_id=1, replica_groups=mesh['freq'=2,'gx'=4,'gy'=2,'col'=2] {'gy','col'}, use_global_device_ids=true, to_apply=%region_5.6 | all-reduce | flops 6 | bytes 48 | tf_op jit(solution)/shard_map/psum | solution.py:123
  132.3 10.7 %psum.38 = f32[6]{0:T(128)S(1)} all-reduce(f32[6]{0:T(128)S(1)} %psum.37), channel_id=1, replica_groups=mesh['freq'=2,'gx'=4,'gy'=2,'col'=2] {'gx'}, use_global_device_ids=true, to_apply=%region_6.7 | all-reduce | flops 6 | bytes 48 | tf_op jit(solution)/shard_map/psum | solution.py:123
  153.1 2.4 %psum.39 = f32[1,4,4]{2,1,0:T(4,128)S(1)} all-reduce(f32[1,4,4]{2,1,0:T(4,128)S(1)} %bitcast.39), channel_id=1, replica_groups=mesh['freq'=2,'gx'=4,'gy'=2,'col'=2] {'col'}, use_global_device_ids=true, to_apply=%region_10.11 | all-reduce | flops 16 | bytes 128 | tf_op jit(solution)/shard_map/psum | solution.py:165
  155.5 26.0 %all_gather.3 = f32[8,4,4]{2,1,0:T(4,128)S(1)} all-gather(f32[1,4,4]{2,1,0:T(4,128)S(1)} %psum.39), channel_id=1, replica_groups=mesh['freq'=2,'gx'=4,'gy'=2,'col'=2] {'gx','gy'}, dimensions={0}, use_global_device_ids=true | all-gather | bytes 576 | tf_op jit(solution)/shard_map/all_gather | solution.py:166
  (141 shorter events, 52.2 us)
Async XLA Ops:
  0.6 31.0 %copy-start.32 = (bf16[16,16,128]{2,1,0:T(8,128)(2,1)S(1)}, bf16[16,16,128]{2,1,0:T(8,128)(2,1)}, u32[]{:S(2)}) copy-start(bf16[16,16,128]{2,1,0:T(8,128)(2,1)} %param.12) | copy-start | bytes 196612
  1.4 31.1 %collective-permute-start = (f32[6,1,16,128]{3,2,1,0:T(8,128)S(1)}, f32[6,1,16,128]{3,2,1,0:T(8,128)S(1)}, u32[]{:S(2)}, u32[]{:S(2)}) collective-permute-start(f32[6,1,16,128]{3,2,1,0:T(8,128)S(1)} %get-tuple-element.41), channel_id=1, source_target_pairs={{4,0},{8,4},{12,8},{5,1},{9,5},{13,9},{6,2},{10,6},{14,10},{7,3},{... | collective-permute-start | bytes 147464 | tf_op jit(solution)/shard_map/ppermute | solution.py:18
  2.7 29.8 %collective-permute-start.1 = (f32[6,1,16,128]{3,2,1,0:T(8,128)S(1)}, f32[6,1,16,128]{3,2,1,0:T(8,128)S(1)}, u32[]{:S(2)}, u32[]{:S(2)}) collective-permute-start(f32[6,1,16,128]{3,2,1,0:T(8,128)S(1)} %get-tuple-element.40), channel_id=1, source_target_pairs={{0,4},{4,8},{8,12},{1,5},{5,9},{9,13},{2,6},{6,10},{10,14},{3,7},{... | collective-permute-start | bytes 147464 | tf_op jit(solution)/shard_map/ppermute | solution.py:17
  12.9 19.5 %copy-start.33 = (s32[1,256]{1,0:T(1,128)S(1)}, s32[1,256]{1,0:T(1,128)}, u32[]{:S(2)}) copy-start(s32[1,256]{1,0:T(1,128)} %param.15) | copy-start | bytes 3076
  12.9 19.5 %copy-start.27 = (bf16[6,16,16,128]{3,2,1,0:T(8,128)(2,1)S(1)}, bf16[6,16,16,128]{3,2,1,0:T(8,128)(2,1)}, u32[]{:S(2)}) copy-start(bf16[6,16,16,128]{3,2,1,0:T(8,128)(2,1)} %param.10) | copy-start | bytes 1179652
  31.6 8.0 %copy-start.34 = (f32[2,3]{1,0:T(2,128)S(1)}, f32[2,3]{1,0:T(2,128)}, u32[]{:S(2)}) copy-start(f32[2,3]{1,0:T(2,128)} %param.16) | copy-start | bytes 76
  32.6 10.9 %collective-permute-start.2 = (f32[6,18,1,128]{3,2,1,0:T(1,128)S(1)}, f32[6,18,1,128]{3,2,1,0:T(1,128)}, u32[]{:S(2)}, u32[]{:S(2)}) collective-permute-start(f32[6,18,1,128]{3,2,1,0:T(1,128)S(1)} %get-tuple-element.35), channel_id=1, source_target_pairs={{2,0},{3,1},{6,4},{7,5},{10,8},{11,9},{14,12},{15,13},{18,16},{19,... | collective-permute-start | bytes 165896 | tf_op jit(solution)/shard_map/ppermute | solution.py:18
  33.9 9.6 %collective-permute-start.3 = (f32[6,18,1,128]{3,2,1,0:T(1,128)S(1)}, f32[6,18,1,128]{3,2,1,0:T(1,128)}, u32[]{:S(2)}, u32[]{:S(2)}) collective-permute-start(f32[6,18,1,128]{3,2,1,0:T(1,128)S(1)} %get-tuple-element.34), channel_id=1, source_target_pairs={{0,2},{1,3},{4,6},{5,7},{8,10},{9,11},{12,14},{13,15},{16,18},{17,... | collective-permute-start | bytes 165896 | tf_op jit(solution)/shard_map/ppermute | solution.py:17
  46.6 8.5 %collective-permute-start.4 = (f32[6,18,18,1]{2,1,3,0:T(8,128)}, f32[6,18,18,1]{2,1,3,0:T(8,128)S(1)}, u32[]{:S(2)}, u32[]{:S(2)}) collective-permute-start(f32[6,18,18,1]{2,1,3,0:T(8,128)} %copy.44), channel_id=1, source_target_pairs={{1,0},{3,2},{5,4},{7,6},{9,8},{11,10},{13,12},{15,14},{17,16},{19,... | collective-permute-start | bytes 23336 | tf_op jit(solution)/shard_map/ppermute | solution.py:18
  48.8 7.0 %collective-permute-start.5 = (f32[6,18,18,1]{2,1,3,0:T(8,128)S(1)}, f32[6,18,18,1]{2,1,3,0:T(8,128)}, u32[]{:S(2)}, u32[]{:S(2)}) collective-permute-start(f32[6,18,18,1]{2,1,3,0:T(8,128)S(1)} %copy.46), channel_id=1, source_target_pairs={{0,1},{2,3},{4,5},{6,7},{8,9},{10,11},{12,13},{14,15},{16,17},{18,... | collective-permute-start | bytes 23336 | tf_op jit(solution)/shard_map/ppermute | solution.py:17
  57.5 3.1 %copy-start.28 = (bf16[6,16,16,128]{3,2,1,0:T(8,128)(2,1)S(1)}, bf16[6,16,16,128]{3,2,1,0:T(8,128)(2,1)}, u32[]{:S(2)}) copy-start(bf16[6,16,16,128]{3,2,1,0:T(8,128)(2,1)} %param.10) | copy-start | bytes 1179652
  82.7 6.1 %copy-start.2 = (f32[1,16,16,128]{3,2,1,0:T(8,128)}, f32[1,16,16,128]{3,2,1,0:T(8,128)S(1)}, u32[]{:S(2)}) copy-start(f32[1,16,16,128]{3,2,1,0:T(8,128)S(1)} %get-tuple-element.15) | copy-start | bytes 393220
  91.5 13.9 %copy-start.31 = (bf16[6,16,16,128]{3,2,1,0:T(8,128)(2,1)S(1)}, bf16[6,16,16,128]{3,2,1,0:T(8,128)(2,1)}, u32[]{:S(2)}) copy-start(bf16[6,16,16,128]{3,2,1,0:T(8,128)(2,1)} %param.11) | copy-start | bytes 1179652
  91.5 6.1 %collective-permute-start.6 = (f32[6,1,16,128]{3,2,1,0:T(8,128)S(1)}, f32[6,1,16,128]{3,2,1,0:T(8,128)S(1)}, u32[]{:S(2)}, u32[]{:S(2)}) collective-permute-start(f32[6,1,16,128]{3,2,1,0:T(8,128)S(1)} %get-tuple-element.38), channel_id=1, source_target_pairs={{4,0},{8,4},{12,8},{5,1},{9,5},{13,9},{6,2},{10,6},{14,10},{7,3},{... | collective-permute-start | bytes 147464 | tf_op jit(solution)/shard_map/ppermute | solution.py:18
  93.0 6.3 %collective-permute-start.7 = (f32[6,1,16,128]{3,2,1,0:T(8,128)S(1)}, f32[6,1,16,128]{3,2,1,0:T(8,128)S(1)}, u32[]{:S(2)}, u32[]{:S(2)}) collective-permute-start(f32[6,1,16,128]{3,2,1,0:T(8,128)S(1)} %get-tuple-element.37), channel_id=1, source_target_pairs={{0,4},{4,8},{8,12},{1,5},{5,9},{9,13},{2,6},{6,10},{10,14},{3,7},{... | collective-permute-start | bytes 147464 | tf_op jit(solution)/shard_map/ppermute | solution.py:17
  99.3 7.0 %collective-permute-start.8 = (f32[6,18,1,128]{3,2,1,0:T(1,128)S(1)}, f32[6,18,1,128]{3,2,1,0:T(1,128)S(1)}, u32[]{:S(2)}, u32[]{:S(2)}) collective-permute-start(f32[6,18,1,128]{3,2,1,0:T(1,128)S(1)} %get-tuple-element.31), channel_id=1, source_target_pairs={{2,0},{3,1},{6,4},{7,5},{10,8},{11,9},{14,12},{15,13},{18,16},{19,... | collective-permute-start | bytes 165896 | tf_op jit(solution)/shard_map/ppermute | solution.py:18
  100.6 6.3 %collective-permute-start.9 = (f32[6,18,1,128]{3,2,1,0:T(1,128)S(1)}, f32[6,18,1,128]{3,2,1,0:T(1,128)S(1)}, u32[]{:S(2)}, u32[]{:S(2)}) collective-permute-start(f32[6,18,1,128]{3,2,1,0:T(1,128)S(1)} %get-tuple-element.30), channel_id=1, source_target_pairs={{0,2},{1,3},{4,6},{5,7},{8,10},{9,11},{12,14},{13,15},{16,18},{17,... | collective-permute-start | bytes 165896 | tf_op jit(solution)/shard_map/ppermute | solution.py:17
  109.8 6.0 %copy-start.11 = (f32[6,18,1,128]{3,2,1,0:T(1,128)S(1)}, f32[6,18,1,128]{3,2,1,0:T(1,128)}, u32[]{:S(2)}) copy-start(f32[6,18,1,128]{3,2,1,0:T(1,128)} %copy-done.10) | copy-start | bytes 165892
  109.8 6.0 %copy-start.14 = (f32[6,18,1,128]{3,2,1,0:T(1,128)S(1)}, f32[6,18,1,128]{3,2,1,0:T(1,128)}, u32[]{:S(2)}) copy-start(f32[6,18,1,128]{3,2,1,0:T(1,128)} %copy-done.13) | copy-start | bytes 165892
  109.8 7.8 %collective-permute-start.10 = (f32[6,18,18,1]{2,1,3,0:T(8,128)}, f32[6,18,18,1]{2,1,3,0:T(8,128)S(1)}, u32[]{:S(2)}, u32[]{:S(2)}) collective-permute-start(f32[6,18,18,1]{2,1,3,0:T(8,128)} %copy.48), channel_id=1, source_target_pairs={{1,0},{3,2},{5,4},{7,6},{9,8},{11,10},{13,12},{15,14},{17,16},{19,... | collective-permute-start | bytes 23336 | tf_op jit(solution)/shard_map/ppermute | solution.py:18
  112.2 6.2 %collective-permute-start.11 = (f32[6,18,18,1]{2,1,3,0:T(8,128)S(1)}, f32[6,18,18,1]{2,1,3,0:T(8,128)}, u32[]{:S(2)}, u32[]{:S(2)}) collective-permute-start(f32[6,18,18,1]{2,1,3,0:T(8,128)S(1)} %copy.50), channel_id=1, source_target_pairs={{0,1},{2,3},{4,5},{6,7},{8,9},{10,11},{12,13},{14,15},{16,17},{18,... | collective-permute-start | bytes 23336 | tf_op jit(solution)/shard_map/ppermute | solution.py:17
  120.0 3.7 %copy-start.8 = (f32[32768]{0:T(1024)S(1)}, f32[32768]{0:T(1024)}, u32[]{:S(2)}) copy-start(f32[32768]{0:T(1024)} %scatter_custom_fusion) | copy-start | bytes 393220
  120.0 3.7 %copy-start.18 = (f32[6,18,17,128]{3,2,1,0:T(8,128)S(1)}, f32[6,18,17,128]{3,2,1,0:T(8,128)}, u32[]{:S(2)}) copy-start(f32[6,18,17,128]{3,2,1,0:T(8,128)} %get-tuple-element.28) | copy-start | bytes 2820100
  120.0 3.7 %copy-start.19 = (f32[6,18,17,128]{3,2,1,0:T(8,128)S(1)}, f32[6,18,17,128]{3,2,1,0:T(8,128)}, u32[]{:S(2)}) copy-start(f32[6,18,17,128]{3,2,1,0:T(8,128)} %get-tuple-element.29) | copy-start | bytes 2820100
  (23 other events, 41.7 us)
